TPU v7x, 32 devices: a whole 2x2x4 slice. The times are simulated.
32 devices in a mesh: lines: 2 (over x), col: 16 (over z, y, core).
Axes of the slice: x: 2, y: 2, z: 4, core: 2. Of those that a mesh axis runs over, the one named last changes fastest.
Arguments:
- primary: float32 [16, 4, 128, 256], P(None, 'lines', 'col'), parts along dimension 1, may hold values from -6 to 6
- conductivity: float32 [128, 512], P('col', 'lines'), parts along dimension 1, may hold values from 0.1 to 10
- wavenumbers: float32 [16], replicated, may hold values from 0.05 to 1.5
- quadrature: float32 [16], replicated, may hold values from 0.02 to 0.2
- electrodes: int32 [64], P(('lines', 'col')), parts along dimension 0, may hold values from 0 to 127, as said below
- far_pole: int32 [4, 32], P('lines'), parts along dimension 0, may hold values from 0 to 31, as said below
- observed: float32 [4, 32], P('lines'), parts along dimension 0, may hold values from -6 to 6
- prior_adjoint: float32 [16, 4, 128, 256], P(None, 'lines', 'col'), parts along dimension 1, may hold values from -0.012 to 0.012
Outputs:
- predicted: float32 [4, 32], P('lines'), parts along dimension 0
- gradient: float32 [128, 512], P('col', 'lines'), parts along dimension 1
There are 2 independent parts, one for each index of `lines`. A program takes and returns all parts, laid end to end along the dimension named above; an argument that names none is the same for every part. Nothing has to cross between parts.
Inputs may be any that keep to these rules, and one draw needn't show every extreme that they name: electrodes[e] lies in columns 4 e to 4 e + 3. far_pole[s, r] differs from r by 1 to 8.
All inputs are finite; a program needn't handle non-finite values.
Results may differ from a plain program's by a relative error of at most 0.0003.
Values sent between devices are 32-bit elements; how exact they have to be, the bound alone decides.
No kernel may reach another device: no remote copies, remote signals or barrier semaphores. Data moves between devices by JAX's collectives and lax.ppermute only.
A program may use at most 64 MiB of HBM per device.

v0:
```python
import jax
import jax.numpy as jnp
from jax import lax
from jax.sharding import PartitionSpec as P

ITERS = 2


def padded_2(block, sides, width):
    for axis, dim in sides:
        count = lax.axis_size(axis)
        forward = [(i, i + 1) for i in range(count - 1)]
        backward = [(target, source) for source, target in forward]
        low = lax.ppermute(
            lax.slice_in_dim(block, block.shape[dim] - width, None, axis=dim), axis, forward
        )
        high = lax.ppermute(lax.slice_in_dim(block, 0, width, axis=dim), axis, backward)
        block = jnp.concatenate([low, block, high], axis=dim)
    return block


def shifted(value, axis, steps):
    count = lax.axis_size(axis)
    initial, last = (max(0, -steps), min(count, count - steps))
    return lax.ppermute(value, axis, [(source, source + steps) for source in range(initial, last)])


def coefficients(sigma_wide):
    center = sigma_wide[1:-1]
    west_face = 0.5 * (center + sigma_wide[:-2])
    east_face = 0.5 * (center + sigma_wide[2:])
    below_sigma = jnp.concatenate([center[:, 1:], jnp.zeros_like(center[:, :1])], axis=1)
    lower_face = 0.5 * (center + below_sigma)
    above_sigma = jnp.concatenate([jnp.zeros_like(center[:, :1]), center[:, :-1]], axis=1)
    upper_face = 0.5 * (center + above_sigma)
    top_row = jnp.arange(center.shape[1]) == 0
    upper_face = jnp.where(top_row[None, :], 0.0, upper_face)
    return (west_face, east_face, lower_face, upper_face, center)


def stencil(field_wide, faces_set, mass_scale):
    west_face, east_face, lower_face, upper_face, center = faces_set
    middle = field_wide[..., 1:-1, :]
    below_cells = jnp.concatenate([middle[..., 1:], jnp.zeros_like(middle[..., :1])], axis=-1)
    above_cells = jnp.concatenate([jnp.zeros_like(middle[..., :1]), middle[..., :-1]], axis=-1)
    result = west_face * (middle - field_wide[..., :-2, :]) + east_face * (
        middle - field_wide[..., 2:, :]
    )
    result = result + lower_face * (middle - below_cells) + upper_face * (middle - above_cells)
    return result + mass_scale * center * middle


def local_sum(left_field, right_field):
    return jnp.sum(left_field * right_field, axis=(2, 3))


def squares(residual):
    return lax.psum(local_sum(residual, residual), "col")


def expand(scalars):
    return scalars[:, :, None, None]


def conjugate(source, first_image, operate, start):
    solution = start
    residual = source
    direction = source
    norm_now = squares(residual)
    applied = first_image
    for iteration in range(ITERS):
        if iteration > 0:
            applied = operate(direction)
        step_size = norm_now / lax.psum(local_sum(direction, applied), "col")
        solution = solution + expand(step_size) * direction
        if iteration + 1 < ITERS:
            residual = residual - expand(step_size) * applied
            norm_next = squares(residual)
            direction = residual + expand(norm_next / norm_now) * direction
            norm_now = norm_next
    return solution


def on_device(
    primary, conductivity, wavenumbers, quadrature, electrodes, far_pole, observed, prior_adjoint
):
    columns = conductivity.shape[0]
    depth_cells = conductivity.shape[1]
    device = lax.axis_index("col")
    device_count = lax.axis_size("col")
    offset = device * columns
    wide_sigma = padded_2(conductivity, (("col", 0),), 2)
    positions = offset - 2 + jnp.arange(columns + 4)
    inside = (positions >= 0) & (positions < columns * device_count)
    contrast_wide = jnp.where(inside[:, None], wide_sigma - 1.0, 0.0)
    mass_scale = (wavenumbers * wavenumbers)[:, None, None, None]
    operator_faces = coefficients(wide_sigma[1:-1])

    def operate(state):
        padded = padded_2(state, (("col", 2),), 1)
        return stencil(padded, operator_faces, mass_scale)

    padded_primary = padded_2(primary, (("col", 2),), 1)
    source = -stencil(padded_primary, coefficients(contrast_wide[1:-1]), mass_scale)
    first_image = operate(source)
    secondary = conjugate(source, first_image, operate, jnp.zeros_like(source))
    total_field = primary + secondary
    surface = total_field[:, :, :, 0]
    weighted = jnp.einsum("k,ksc->sc", quadrature, surface, precision=lax.Precision.HIGHEST)
    pick_table = (electrodes[:, None] - offset == jnp.arange(columns)[None, :]).astype(jnp.float32)
    own_potentials = jnp.einsum("sc,ec->se", weighted, pick_table, precision=lax.Precision.HIGHEST)
    potentials = lax.all_gather(own_potentials, "col", axis=1, tiled=True)
    predicted = potentials - jnp.take_along_axis(potentials, far_pole, axis=1)
    misfit = predicted - observed
    own_count = electrodes.shape[0]
    own_ids = device * own_count + jnp.arange(own_count)
    own_misfit = lax.dynamic_slice_in_dim(misfit, device * own_count, own_count, 1)
    far_hits = (far_pole[:, :, None] == own_ids[None, None, :]).astype(jnp.float32)
    returned = jnp.einsum("sr,sre->se", misfit, far_hits, precision=lax.Precision.HIGHEST)
    charge = own_misfit - returned
    charge_cols = jnp.einsum("se,ec->sc", charge, pick_table, precision=lax.Precision.HIGHEST)
    surface_row = (jnp.arange(depth_cells) == 0).astype(jnp.float32)
    adjoint_source = quadrature[:, None, None, None] * charge_cols[None, :, :, None] * surface_row
    adjoint_residual = adjoint_source - operate(prior_adjoint)
    adjoint = conjugate(adjoint_residual, operate(adjoint_residual), operate, prior_adjoint)
    edge_columns = shifted((adjoint[:, :, :1], total_field[:, :, :1]), "col", -1)
    adjoint_next = jnp.concatenate([adjoint[:, :, 1:], edge_columns[0]], axis=2)
    total_next = jnp.concatenate([total_field[:, :, 1:], edge_columns[1]], axis=2)
    adjoint_down = jnp.concatenate([adjoint[..., 1:], jnp.zeros_like(adjoint[..., :1])], axis=-1)
    total_down = jnp.concatenate(
        [total_field[..., 1:], jnp.zeros_like(total_field[..., :1])], axis=-1
    )
    correlation = (adjoint_next - adjoint) * (total_next - total_field)
    correlation = correlation + (adjoint_down - adjoint) * (total_down - total_field)
    correlation = correlation + mass_scale * adjoint * total_field
    gradient = jnp.sum(correlation, axis=(0, 1))
    return (predicted, gradient)


def solution(mesh):
    placed = (
        P(None, "lines", "col", None),
        P("col", "lines"),
        P(),
        P(),
        P(("lines", "col")),
        P("lines", None),
        P("lines", None),
        P(None, "lines", "col", None),
    )
    return jax.shard_map(
        on_device,
        mesh=mesh,
        in_specs=placed,
        out_specs=(P("lines", None), P("col", "lines")),
        check_vma=False,
    )
```

profile of v0, /device:TPU:1, one launch (start us, length us, event | category | flops | bytes accessed | tf_op | source)
XLA Modules:
  0.0 319.6 jit_solution(12586996976462141782)
XLA Ops:
  0.6 0.8 fusion.97
  1.4 1.9 collective-permute-start.1
  3.3 4.5 %collective-permute-start = (f32[2,256]{1,0:T(2,128)S(1)}, f32[2,256]{1,0:T(2,128)S(1)}, u32[]{:S(2)}, u32[]{:S(2)}) collective-permute-start(f32[2,256]{1,0:T(2,128)S(1)} %get-tuple-element.61), channel_id=1, source_target_pairs={{0,1},{1,2},{2,3},{3,4},{4,5},{5,6},{6,7},{7,8},{8,9},{9,10},{10,1... | collective-permute-start | bytes 6152 | tf_op jit(solution)/shard_map/ppermute | solution.py:14
  7.9 1.1 fusion.93
  9.0 1.9 collective-permute-start.3
  10.9 3.6 %collective-permute-start.2 = (f32[16,2,1,256]{3,2,1,0:T(1,128)S(1)}, f32[16,2,1,256]{3,2,1,0:T(1,128)S(1)}, u32[]{:S(2)}, u32[]{:S(2)}) collective-permute-start(f32[16,2,1,256]{3,2,1,0:T(1,128)S(1)} %get-tuple-element.44), channel_id=1, source_target_pairs={{0,1},{1,2},{2,3},{3,4},{4,5},{5,6},{6,7},{7,8},{8,9},{9,10},{10,1... | collective-permute-start | bytes 98312 | tf_op jit(solution)/shard_map/ppermute | solution.py:14
  14.5 1.1 fusion.88
  15.6 1.9 collective-permute-start.9
  20.8 3.6 %collective-permute-start.8 = (f32[16,2,1,256]{3,2,1,0:T(1,128)S(1)}, f32[16,2,1,256]{3,2,1,0:T(1,128)S(1)}, u32[]{:S(2)}, u32[]{:S(2)}) collective-permute-start(f32[16,2,1,256]{3,2,1,0:T(1,128)S(1)} %get-tuple-element.34), channel_id=1, source_target_pairs={{0,1},{1,2},{2,3},{3,4},{4,5},{5,6},{6,7},{7,8},{8,9},{9,10},{10,1... | collective-permute-start | bytes 98312 | tf_op jit(solution)/shard_map/ppermute | solution.py:14
  25.1 1.9 collective-permute-start.5
  27.1 3.6 %collective-permute-start.4 = (f32[16,2,1,256]{3,2,1,0:T(1,128)S(1)}, f32[16,2,1,256]{3,2,1,0:T(1,128)S(1)}, u32[]{:S(2)}, u32[]{:S(2)}) collective-permute-start(f32[16,2,1,256]{3,2,1,0:T(1,128)S(1)} %get-tuple-element.40), channel_id=1, source_target_pairs={{0,1},{1,2},{2,3},{3,4},{4,5},{5,6},{6,7},{7,8},{8,9},{9,10},{10,1... | collective-permute-start | bytes 98312 | tf_op jit(solution)/shard_map/ppermute | solution.py:14
  30.9 0.9 collective-permute-done.4
  32.1 55.7 %all-reduce.19 = (f32[16,2]{1,0:T(8,128)S(1)}, f32[16,2]{1,0:T(8,128)S(1)}) all-reduce(f32[16,2]{1,0:T(8,128)S(1)} %get-tuple-element.13, f32[16,2]{1,0:T(8,128)S(1)} %get-tuple-element.12), channel_id=1, replica_groups=mesh['lines'=2,'col'=16] {'col'}, use_global_device_ids=true, to_apply=%region_1.2 | all-reduce | flops 64 | bytes 512 | tf_op jit(solution)/shard_map/psum | solution.py:58
  88.1 34.4 %psum.58 = f32[16,2]{1,0:T(8,128)S(1)} all-reduce(f32[16,2]{1,0:T(8,128)S(1)} %multiply_reduce_fusion.3), channel_id=1, replica_groups=mesh['lines'=2,'col'=16] {'col'}, use_global_device_ids=true, to_apply=%region_5.6 | all-reduce | flops 32 | bytes 256 | tf_op jit(solution)/shard_map/psum | solution.py:58
  122.7 2.5 collective-permute-start.7
  125.2 3.1 collective-permute-start.6
  128.5 0.9 collective-permute-done.6
  129.7 28.5 %psum.59 = f32[16,2]{1,0:T(8,128)S(1)} all-reduce(f32[16,2]{1,0:T(8,128)S(1)} %fusion.55), channel_id=1, replica_groups=mesh['lines'=2,'col'=16] {'col'}, use_global_device_ids=true, to_apply=%region_7.8 | all-reduce | flops 32 | bytes 256 | tf_op jit(solution)/shard_map/psum | solution.py:74
  159.4 19.0 %all-gather = f32[16,2,2]{2,1,0:T(2,128)S(1)} all-gather(f32[1,2,2]{2,1,0:T(2,128)S(1)} %convolution_bitcast_fusion), channel_id=1, replica_groups=mesh['lines'=2,'col'=16] {'col'}, dimensions={0}, use_global_device_ids=true | all-gather | bytes 272 | tf_op jit(solution)/shard_map/all_gather | solution.py:112
  178.5 0.9 gather_fusion
  181.5 2.1 collective-permute-start.11
  183.6 3.5 %collective-permute-start.10 = (f32[16,2,1,256]{3,2,1,0:T(1,128)S(1)}, f32[16,2,1,256]{3,2,1,0:T(1,128)S(1)}, u32[]{:S(2)}, u32[]{:S(2)}) collective-permute-start(f32[16,2,1,256]{3,2,1,0:T(1,128)S(1)} %get-tuple-element.28), channel_id=1, source_target_pairs={{0,1},{1,2},{2,3},{3,4},{4,5},{5,6},{6,7},{7,8},{8,9},{9,10},{10,1... | collective-permute-start | bytes 98312 | tf_op jit(solution)/shard_map/ppermute | solution.py:14
  187.2 1.9 collective-permute-start.15
  189.6 53.5 %all-reduce.18 = (f32[16,2]{1,0:T(8,128)S(1)}, f32[16,2]{1,0:T(8,128)S(1)}) all-reduce(f32[16,2]{1,0:T(8,128)S(1)} %get-tuple-element.11, f32[16,2]{1,0:T(8,128)S(1)} %get-tuple-element.10), channel_id=1, replica_groups=mesh['lines'=2,'col'=16] {'col'}, use_global_device_ids=true, to_apply=%region_9.10 | all-reduce | flops 64 | bytes 512 | tf_op jit(solution)/shard_map/psum | solution.py:58
  243.3 34.4 %psum.62 = f32[16,2]{1,0:T(8,128)S(1)} all-reduce(f32[16,2]{1,0:T(8,128)S(1)} %multiply_reduce_fusion), channel_id=1, replica_groups=mesh['lines'=2,'col'=16] {'col'}, use_global_device_ids=true, to_apply=%region_13.14 | all-reduce | flops 32 | bytes 256 | tf_op jit(solution)/shard_map/psum | solution.py:58
  277.9 2.5 collective-permute-start.13
  280.5 3.1 collective-permute-start.12
  283.7 0.9 collective-permute-done.12
  284.9 28.5 %psum.63 = f32[16,2]{1,0:T(8,128)S(1)} all-reduce(f32[16,2]{1,0:T(8,128)S(1)} %fusion.56), channel_id=1, replica_groups=mesh['lines'=2,'col'=16] {'col'}, use_global_device_ids=true, to_apply=%region_15.16 | all-reduce | flops 32 | bytes 256 | tf_op jit(solution)/shard_map/psum | solution.py:74
  313.6 3.9 %collective-permute-start.14 = (f32[16,2,1,256]{3,2,1,0:T(1,128)S(1)}, f32[16,2,1,256]{3,2,1,0:T(1,128)S(1)}, u32[]{:S(2)}, u32[]{:S(2)}) collective-permute-start(f32[16,2,1,256]{3,2,1,0:T(1,128)S(1)} %slice.266), channel_id=1, source_target_pairs={{1,0},{2,1},{3,2},{4,3},{5,4},{6,5},{7,6},{8,7},{9,8},{10,9},{11,1... | collective-permute-start | bytes 98312 | tf_op jit(solution)/shard_map/ppermute | solution.py:25
  317.8 1.0 collective-permute-done.14
  318.8 0.8 fusion.54
  (86 shorter events, 10.5 us)
Async XLA Ops:
  0.6 16.9 %copy-start = (f32[16,2,8,256]{3,2,1,0:T(8,128)S(1)}, f32[16,2,8,256]{3,2,1,0:T(8,128)}, u32[]{:S(2)}) copy-start(f32[16,2,8,256]{3,2,1,0:T(8,128)} %param.8) | copy-start | bytes 786436
  1.4 19.4 %collective-permute-start.1 = (f32[2,256]{1,0:T(2,128)S(1)}, f32[2,256]{1,0:T(2,128)S(1)}, u32[]{:S(2)}, u32[]{:S(2)}) collective-permute-start(f32[2,256]{1,0:T(2,128)S(1)} %get-tuple-element.62), channel_id=1, source_target_pairs={{1,0},{2,1},{3,2},{4,3},{5,4},{6,5},{7,6},{8,7},{9,8},{10,9},{11,1... | collective-permute-start | bytes 6152 | tf_op jit(solution)/shard_map/ppermute | solution.py:17
  3.3 21.1 %collective-permute-start = (f32[2,256]{1,0:T(2,128)S(1)}, f32[2,256]{1,0:T(2,128)S(1)}, u32[]{:S(2)}, u32[]{:S(2)}) collective-permute-start(f32[2,256]{1,0:T(2,128)S(1)} %get-tuple-element.61), channel_id=1, source_target_pairs={{0,1},{1,2},{2,3},{3,4},{4,5},{5,6},{6,7},{7,8},{8,9},{9,10},{10,1... | collective-permute-start | bytes 6152 | tf_op jit(solution)/shard_map/ppermute | solution.py:14
  9.0 15.9 %collective-permute-start.3 = (f32[16,2,1,256]{3,2,1,0:T(1,128)S(1)}, f32[16,2,1,256]{3,2,1,0:T(1,128)S(1)}, u32[]{:S(2)}, u32[]{:S(2)}) collective-permute-start(f32[16,2,1,256]{3,2,1,0:T(1,128)S(1)} %get-tuple-element.45), channel_id=1, source_target_pairs={{1,0},{2,1},{3,2},{4,3},{5,4},{6,5},{7,6},{8,7},{9,8},{10,9},{11,1... | collective-permute-start | bytes 98312 | tf_op jit(solution)/shard_map/ppermute | solution.py:17
  10.9 14.0 %collective-permute-start.2 = (f32[16,2,1,256]{3,2,1,0:T(1,128)S(1)}, f32[16,2,1,256]{3,2,1,0:T(1,128)S(1)}, u32[]{:S(2)}, u32[]{:S(2)}) collective-permute-start(f32[16,2,1,256]{3,2,1,0:T(1,128)S(1)} %get-tuple-element.44), channel_id=1, source_target_pairs={{0,1},{1,2},{2,3},{3,4},{4,5},{5,6},{6,7},{7,8},{8,9},{9,10},{10,1... | collective-permute-start | bytes 98312 | tf_op jit(solution)/shard_map/ppermute | solution.py:14
  15.6 165.5 %collective-permute-start.9 = (f32[16,2,1,256]{3,2,1,0:T(1,128)S(1)}, f32[16,2,1,256]{3,2,1,0:T(1,128)S(1)}, u32[]{:S(2)}, u32[]{:S(2)}) collective-permute-start(f32[16,2,1,256]{3,2,1,0:T(1,128)S(1)} %get-tuple-element.35), channel_id=1, source_target_pairs={{1,0},{2,1},{3,2},{4,3},{5,4},{6,5},{7,6},{8,7},{9,8},{10,9},{11,1... | collective-permute-start | bytes 98312 | tf_op jit(solution)/shard_map/ppermute | solution.py:17
  17.6 0.7 copy-start.2
  17.6 1.0 copy-start.1
  18.7 0.7 copy-start.6
  19.4 0.7 copy-start.3
  20.0 0.7 copy-start.7
  20.8 160.3 %collective-permute-start.8 = (f32[16,2,1,256]{3,2,1,0:T(1,128)S(1)}, f32[16,2,1,256]{3,2,1,0:T(1,128)S(1)}, u32[]{:S(2)}, u32[]{:S(2)}) collective-permute-start(f32[16,2,1,256]{3,2,1,0:T(1,128)S(1)} %get-tuple-element.34), channel_id=1, source_target_pairs={{0,1},{1,2},{2,3},{3,4},{4,5},{5,6},{6,7},{7,8},{8,9},{9,10},{10,1... | collective-permute-start | bytes 98312 | tf_op jit(solution)/shard_map/ppermute | solution.py:14
  25.1 5.7 %collective-permute-start.5 = (f32[16,2,1,256]{3,2,1,0:T(1,128)S(1)}, f32[16,2,1,256]{3,2,1,0:T(1,128)S(1)}, u32[]{:S(2)}, u32[]{:S(2)}) collective-permute-start(f32[16,2,1,256]{3,2,1,0:T(1,128)S(1)} %get-tuple-element.41), channel_id=1, source_target_pairs={{1,0},{2,1},{3,2},{4,3},{5,4},{6,5},{7,6},{8,7},{9,8},{10,9},{11,1... | collective-permute-start | bytes 98312 | tf_op jit(solution)/shard_map/ppermute | solution.py:17
  27.1 4.7 %collective-permute-start.4 = (f32[16,2,1,256]{3,2,1,0:T(1,128)S(1)}, f32[16,2,1,256]{3,2,1,0:T(1,128)S(1)}, u32[]{:S(2)}, u32[]{:S(2)}) collective-permute-start(f32[16,2,1,256]{3,2,1,0:T(1,128)S(1)} %get-tuple-element.40), channel_id=1, source_target_pairs={{0,1},{1,2},{2,3},{3,4},{4,5},{5,6},{6,7},{7,8},{8,9},{9,10},{10,1... | collective-permute-start | bytes 98312 | tf_op jit(solution)/shard_map/ppermute | solution.py:14
  122.7 5.7 %collective-permute-start.7 = (f32[16,2,1,256]{3,2,1,0:T(1,128)S(1)}, f32[16,2,1,256]{3,2,1,0:T(1,128)S(1)}, u32[]{:S(2)}, u32[]{:S(2)}) collective-permute-start(f32[16,2,1,256]{3,2,1,0:T(1,128)S(1)} %get-tuple-element.37), channel_id=1, source_target_pairs={{1,0},{2,1},{3,2},{4,3},{5,4},{6,5},{7,6},{8,7},{9,8},{10,9},{11,1... | collective-permute-start | bytes 98312 | tf_op jit(solution)/shard_map/ppermute | solution.py:17
  125.2 4.1 %collective-permute-start.6 = (f32[16,2,1,256]{3,2,1,0:T(1,128)S(1)}, f32[16,2,1,256]{3,2,1,0:T(1,128)S(1)}, u32[]{:S(2)}, u32[]{:S(2)}) collective-permute-start(f32[16,2,1,256]{3,2,1,0:T(1,128)S(1)} %get-tuple-element.36), channel_id=1, source_target_pairs={{0,1},{1,2},{2,3},{3,4},{4,5},{5,6},{6,7},{7,8},{8,9},{9,10},{10,1... | collective-permute-start | bytes 98312 | tf_op jit(solution)/shard_map/ppermute | solution.py:14
  158.4 0.7 copy-start.4
  179.4 0.7 copy-start.5
  181.5 7.7 %collective-permute-start.11 = (f32[16,2,1,256]{3,2,1,0:T(1,128)S(1)}, f32[16,2,1,256]{3,2,1,0:T(1,128)S(1)}, u32[]{:S(2)}, u32[]{:S(2)}) collective-permute-start(f32[16,2,1,256]{3,2,1,0:T(1,128)S(1)} %get-tuple-element.29), channel_id=1, source_target_pairs={{1,0},{2,1},{3,2},{4,3},{5,4},{6,5},{7,6},{8,7},{9,8},{10,9},{11,1... | collective-permute-start | bytes 98312 | tf_op jit(solution)/shard_map/ppermute | solution.py:17
  183.6 5.6 %collective-permute-start.10 = (f32[16,2,1,256]{3,2,1,0:T(1,128)S(1)}, f32[16,2,1,256]{3,2,1,0:T(1,128)S(1)}, u32[]{:S(2)}, u32[]{:S(2)}) collective-permute-start(f32[16,2,1,256]{3,2,1,0:T(1,128)S(1)} %get-tuple-element.28), channel_id=1, source_target_pairs={{0,1},{1,2},{2,3},{3,4},{4,5},{5,6},{6,7},{7,8},{8,9},{9,10},{10,1... | collective-permute-start | bytes 98312 | tf_op jit(solution)/shard_map/ppermute | solution.py:14
  187.2 130.6 %collective-permute-start.15 = (f32[16,2,1,256]{3,2,1,0:T(1,128)S(1)}, f32[16,2,1,256]{3,2,1,0:T(1,128)S(1)}, u32[]{:S(2)}, u32[]{:S(2)}) collective-permute-start(f32[16,2,1,256]{3,2,1,0:T(1,128)S(1)} %slice.268), channel_id=1, source_target_pairs={{1,0},{2,1},{3,2},{4,3},{5,4},{6,5},{7,6},{8,7},{9,8},{10,9},{11,1... | collective-permute-start | bytes 98312 | tf_op jit(solution)/shard_map/ppermute | solution.py:25
  277.9 5.7 %collective-permute-start.13 = (f32[16,2,1,256]{3,2,1,0:T(1,128)S(1)}, f32[16,2,1,256]{3,2,1,0:T(1,128)S(1)}, u32[]{:S(2)}, u32[]{:S(2)}) collective-permute-start(f32[16,2,1,256]{3,2,1,0:T(1,128)S(1)} %get-tuple-element.25), channel_id=1, source_target_pairs={{1,0},{2,1},{3,2},{4,3},{5,4},{6,5},{7,6},{8,7},{9,8},{10,9},{11,1... | collective-permute-start | bytes 98312 | tf_op jit(solution)/shard_map/ppermute | solution.py:17
  280.5 4.1 %collective-permute-start.12 = (f32[16,2,1,256]{3,2,1,0:T(1,128)S(1)}, f32[16,2,1,256]{3,2,1,0:T(1,128)S(1)}, u32[]{:S(2)}, u32[]{:S(2)}) collective-permute-start(f32[16,2,1,256]{3,2,1,0:T(1,128)S(1)} %get-tuple-element.24), channel_id=1, source_target_pairs={{0,1},{1,2},{2,3},{3,4},{4,5},{5,6},{6,7},{7,8},{8,9},{9,10},{10,1... | collective-permute-start | bytes 98312 | tf_op jit(solution)/shard_map/ppermute | solution.py:14
  313.6 5.2 %collective-permute-start.14 = (f32[16,2,1,256]{3,2,1,0:T(1,128)S(1)}, f32[16,2,1,256]{3,2,1,0:T(1,128)S(1)}, u32[]{:S(2)}, u32[]{:S(2)}) collective-permute-start(f32[16,2,1,256]{3,2,1,0:T(1,128)S(1)} %slice.266), channel_id=1, source_target_pairs={{1,0},{2,1},{3,2},{4,3},{5,4},{6,5},{7,6},{8,7},{9,8},{10,9},{11,1... | collective-permute-start | bytes 98312 | tf_op jit(solution)/shard_map/ppermute | solution.py:25
where the time goes:
time: 320 us
  blocking collectives  254 us (79%)
  starting transfers between devices  45.6 us (14%)
  local copies, waits for them, and re-layouts  9.47 us (3%)
  other arithmetic  4.88 us (2%)
  waiting for transfers between devices  3.57 us (1%)
    psum x4, blocking collectives, squares(): return lax.psum(local_sum(residual, residual), 'col')  178 us
    psum x2, blocking collectives, conjugate(): step_size = norm_now / lax.psum(local_sum(direction, applied), 'col')  57 us
    ppermute x7, starting transfers between devices, padded_2(): lax.ppermute(lax.slice_in_dim(block, block.shape[dim] - width, None, axis...  25.1 us
    all_gather x1, blocking collectives, on_device(): potentials = lax.all_gather(own_potentials, 'col', axis=1, tiled=True)  19 us
    ppermute x7, starting transfers between devices, padded_2(): lax.ppermute(lax.slice_in_dim(block, 0, width, axis=dim), axis, backward)  14.8 us
  transfers between devices with their start and end apart: 16, of which 4 were waited for; matrix products, arithmetic and copies ran while one was open for 3% of the time, Pallas kernels for 0%

commit v1 on v0

--- a/solution.py
+++ b/solution.py
@@ -71,7 +71,7 @@
     for iteration in range(ITERS):
         if iteration > 0:
             applied = operate(direction)
-        step_size = norm_now / lax.psum(local_sum(direction, applied), "col")
+        step_size = norm_now / jnp.sum(lax.all_gather(local_sum(direction, applied), "col"), axis=0)
         solution = solution + expand(step_size) * direction
         if iteration + 1 < ITERS:
             residual = residual - expand(step_size) * applied

time: 320 us -> 282 us (0.88)
  blocking collectives: 254 us -> 213 us
    all_gather x0 -> x4, blocking collectives: none -> 78.4 us  [conjugate(): lax.all_gather(local_sum(direction, applied), 'col')]
    psum x4, blocking collectives: 178 us -> 117 us  [squares(): return lax.psum(local_sum(residual, residual), 'col')]
    psum x2 -> x0, blocking collectives: 57 us -> none  [conjugate(): step_size = norm_now / lax.psum(local_sum(direction, applied), 'col')]
    ppermute x7, starting transfers between devices: 14.8 us -> 18.8 us  [padded_2(): lax.ppermute(lax.slice_in_dim(block, 0, width, axis=dim), axis, backward)]
  transfers between devices with their start and end apart: 16 -> 16, of which waited for: 4 -> 4; matrix products, arithmetic and copies ran while one was open for 3% -> 4% of each run, Pallas kernels for 0% -> 0%
where the time goes in v1:
time: 282 us
  blocking collectives  213 us (76%)
  starting transfers between devices  45.6 us (16%)
  local copies, waits for them, and re-layouts  10.1 us (4%)
  waiting for transfers between devices  5.74 us (2%)
  other arithmetic  5.02 us (2%)
    psum x4, blocking collectives, squares(): return lax.psum(local_sum(residual, residual), 'col')  117 us
    all_gather x4, blocking collectives, conjugate(): lax.all_gather(local_sum(direction, applied), 'col')  78.4 us
    ppermute x7, starting transfers between devices, padded_2(): lax.ppermute(lax.slice_in_dim(block, block.shape[dim] - width, None, axis...  22.8 us
    ppermute x7, starting transfers between devices, padded_2(): lax.ppermute(lax.slice_in_dim(block, 0, width, axis=dim), axis, backward)  18.8 us
    all_gather x1, blocking collectives, on_device(): potentials = lax.all_gather(own_potentials, 'col', axis=1, tiled=True)  17.5 us
  transfers between devices with their start and end apart: 16, of which 4 were waited for; matrix products, arithmetic and copies ran while one was open for 4% of the time, Pallas kernels for 0%

profile of v1, /device:TPU:1, one launch (start us, length us, event | category | flops | bytes accessed | tf_op | source)
XLA Modules:
  0.0 281.7 jit_solution(9320839059144562574)
XLA Ops:
  1.4 1.9 collective-permute-start.1
  3.3 4.5 %collective-permute-start = (f32[2,256]{1,0:T(2,128)S(1)}, f32[2,256]{1,0:T(2,128)S(1)}, u32[]{:S(2)}, u32[]{:S(2)}) collective-permute-start(f32[2,256]{1,0:T(2,128)S(1)} %get-tuple-element.61), channel_id=1, source_target_pairs={{0,1},{1,2},{2,3},{3,4},{4,5},{5,6},{6,7},{7,8},{8,9},{9,10},{10,1... | collective-permute-start | bytes 6152 | tf_op jit(solution)/shard_map/ppermute | solution.py:14
  7.9 1.1 fusion.93
  9.0 1.9 collective-permute-start.3
  10.9 3.6 %collective-permute-start.2 = (f32[16,2,1,256]{3,2,1,0:T(1,128)S(1)}, f32[16,2,1,256]{3,2,1,0:T(1,128)S(1)}, u32[]{:S(2)}, u32[]{:S(2)}) collective-permute-start(f32[16,2,1,256]{3,2,1,0:T(1,128)S(1)} %get-tuple-element.44), channel_id=1, source_target_pairs={{0,1},{1,2},{2,3},{3,4},{4,5},{5,6},{6,7},{7,8},{8,9},{9,10},{10,1... | collective-permute-start | bytes 98312 | tf_op jit(solution)/shard_map/ppermute | solution.py:14
  14.5 1.1 fusion.88
  15.6 1.9 collective-permute-start.9
  20.8 3.6 %collective-permute-start.8 = (f32[16,2,1,256]{3,2,1,0:T(1,128)S(1)}, f32[16,2,1,256]{3,2,1,0:T(1,128)S(1)}, u32[]{:S(2)}, u32[]{:S(2)}) collective-permute-start(f32[16,2,1,256]{3,2,1,0:T(1,128)S(1)} %get-tuple-element.34), channel_id=1, source_target_pairs={{0,1},{1,2},{2,3},{3,4},{4,5},{5,6},{6,7},{7,8},{8,9},{9,10},{10,1... | collective-permute-start | bytes 98312 | tf_op jit(solution)/shard_map/ppermute | solution.py:14
  25.1 1.9 collective-permute-start.5
  27.1 3.6 %collective-permute-start.4 = (f32[16,2,1,256]{3,2,1,0:T(1,128)S(1)}, f32[16,2,1,256]{3,2,1,0:T(1,128)S(1)}, u32[]{:S(2)}, u32[]{:S(2)}) collective-permute-start(f32[16,2,1,256]{3,2,1,0:T(1,128)S(1)} %get-tuple-element.40), channel_id=1, source_target_pairs={{0,1},{1,2},{2,3},{3,4},{4,5},{5,6},{6,7},{7,8},{8,9},{9,10},{10,1... | collective-permute-start | bytes 98312 | tf_op jit(solution)/shard_map/ppermute | solution.py:14
  30.9 0.9 collective-permute-done.4
  32.1 30.8 %psum.28 = f32[16,2]{1,0:T(8,128)S(1)} all-reduce(f32[16,2]{1,0:T(8,128)S(1)} %get-tuple-element.17), channel_id=1, replica_groups=mesh['lines'=2,'col'=16] {'col'}, use_global_device_ids=true, to_apply=%region_1.2 | all-reduce | flops 32 | bytes 256 | tf_op jit(solution)/shard_map/psum | solution.py:58
  63.0 19.4 %all-gather.4 = f32[16,16,2]{1,2,0:T(2,128)S(1)} all-gather(f32[1,16,2]{1,2,0:T(2,128)S(1)} %bitcast.31), channel_id=2, replica_groups=mesh['lines'=2,'col'=16] {'col'}, dimensions={0}, use_global_device_ids=true | all-gather | bytes 2176 | tf_op jit(solution)/shard_map/all_gather | solution.py:74
  82.8 29.5 %psum.29 = f32[16,2]{1,0:T(8,128)S(1)} all-reduce(f32[16,2]{1,0:T(8,128)S(1)} %multiply_reduce_fusion.3), channel_id=1, replica_groups=mesh['lines'=2,'col'=16] {'col'}, use_global_device_ids=true, to_apply=%region_5.6 | all-reduce | flops 32 | bytes 256 | tf_op jit(solution)/shard_map/psum | solution.py:58
  112.5 4.5 %collective-permute-start.7 = (f32[16,2,1,256]{3,2,1,0:T(1,128)S(1)}, f32[16,2,1,256]{3,2,1,0:T(1,128)S(1)}, u32[]{:S(2)}, u32[]{:S(2)}) collective-permute-start(f32[16,2,1,256]{3,2,1,0:T(1,128)S(1)} %get-tuple-element.37), channel_id=1, source_target_pairs={{1,0},{2,1},{3,2},{4,3},{5,4},{6,5},{7,6},{8,7},{9,8},{10,9},{11,1... | collective-permute-start | bytes 98312 | tf_op jit(solution)/shard_map/ppermute | solution.py:17
  117.0 1.9 collective-permute-start.6
  119.1 1.0 collective-permute-done.6
  120.5 19.5 %all-gather.5 = f32[16,16,2]{1,2,0:T(2,128)S(1)} all-gather(f32[1,16,2]{1,2,0:T(2,128)S(1)} %bitcast.32), channel_id=3, replica_groups=mesh['lines'=2,'col'=16] {'col'}, dimensions={0}, use_global_device_ids=true | all-gather | bytes 2176 | tf_op jit(solution)/shard_map/all_gather | solution.py:74
  141.4 17.5 %all-gather.6 = f32[16,2,2]{2,1,0:T(2,128)S(1)} all-gather(f32[1,2,2]{2,1,0:T(2,128)S(1)} %convolution_bitcast_fusion), channel_id=1, replica_groups=mesh['lines'=2,'col'=16] {'col'}, dimensions={0}, use_global_device_ids=true | all-gather | bytes 272 | tf_op jit(solution)/shard_map/all_gather | solution.py:112
  158.9 0.9 gather_fusion
  161.9 2.1 collective-permute-start.11
  164.0 3.5 %collective-permute-start.10 = (f32[16,2,1,256]{3,2,1,0:T(1,128)S(1)}, f32[16,2,1,256]{3,2,1,0:T(1,128)S(1)}, u32[]{:S(2)}, u32[]{:S(2)}) collective-permute-start(f32[16,2,1,256]{3,2,1,0:T(1,128)S(1)} %get-tuple-element.28), channel_id=1, source_target_pairs={{0,1},{1,2},{2,3},{3,4},{4,5},{5,6},{6,7},{7,8},{8,9},{9,10},{10,1... | collective-permute-start | bytes 98312 | tf_op jit(solution)/shard_map/ppermute | solution.py:14
  167.7 1.9 collective-permute-start.15
  170.0 27.6 %psum.30 = f32[16,2]{1,0:T(8,128)S(1)} all-reduce(f32[16,2]{1,0:T(8,128)S(1)} %get-tuple-element.15), channel_id=1, replica_groups=mesh['lines'=2,'col'=16] {'col'}, use_global_device_ids=true, to_apply=%region_9.10 | all-reduce | flops 32 | bytes 256 | tf_op jit(solution)/shard_map/psum | solution.py:58
  197.7 20.1 %all-gather.7 = f32[16,16,2]{1,2,0:T(2,128)S(1)} all-gather(f32[1,16,2]{1,2,0:T(2,128)S(1)} %bitcast.33), channel_id=4, replica_groups=mesh['lines'=2,'col'=16] {'col'}, dimensions={0}, use_global_device_ids=true | all-gather | bytes 2176 | tf_op jit(solution)/shard_map/all_gather | solution.py:74
  218.1 29.5 %psum.31 = f32[16,2]{1,0:T(8,128)S(1)} all-reduce(f32[16,2]{1,0:T(8,128)S(1)} %multiply_reduce_fusion), channel_id=1, replica_groups=mesh['lines'=2,'col'=16] {'col'}, use_global_device_ids=true, to_apply=%region_13.14 | all-reduce | flops 32 | bytes 256 | tf_op jit(solution)/shard_map/psum | solution.py:58
  247.8 4.5 %collective-permute-start.13 = (f32[16,2,1,256]{3,2,1,0:T(1,128)S(1)}, f32[16,2,1,256]{3,2,1,0:T(1,128)S(1)}, u32[]{:S(2)}, u32[]{:S(2)}) collective-permute-start(f32[16,2,1,256]{3,2,1,0:T(1,128)S(1)} %get-tuple-element.25), channel_id=1, source_target_pairs={{1,0},{2,1},{3,2},{4,3},{5,4},{6,5},{7,6},{8,7},{9,8},{10,9},{11,1... | collective-permute-start | bytes 98312 | tf_op jit(solution)/shard_map/ppermute | solution.py:17
  252.4 1.9 collective-permute-start.12
  254.4 1.0 collective-permute-done.12
  255.9 19.5 %all-gather.8 = f32[16,16,2]{1,2,0:T(2,128)S(1)} all-gather(f32[1,16,2]{1,2,0:T(2,128)S(1)} %bitcast.34), channel_id=5, replica_groups=mesh['lines'=2,'col'=16] {'col'}, dimensions={0}, use_global_device_ids=true | all-gather | bytes 2176 | tf_op jit(solution)/shard_map/all_gather | solution.py:74
  275.7 2.1 collective-permute-start.14
  278.1 2.8 collective-permute-done.14
  (100 shorter events, 12.9 us)
Async XLA Ops:
  0.6 16.9 %copy-start = (f32[16,2,8,256]{3,2,1,0:T(8,128)S(1)}, f32[16,2,8,256]{3,2,1,0:T(8,128)}, u32[]{:S(2)}) copy-start(f32[16,2,8,256]{3,2,1,0:T(8,128)} %param.8) | copy-start | bytes 786436
  1.4 19.4 %collective-permute-start.1 = (f32[2,256]{1,0:T(2,128)S(1)}, f32[2,256]{1,0:T(2,128)S(1)}, u32[]{:S(2)}, u32[]{:S(2)}) collective-permute-start(f32[2,256]{1,0:T(2,128)S(1)} %get-tuple-element.62), channel_id=1, source_target_pairs={{1,0},{2,1},{3,2},{4,3},{5,4},{6,5},{7,6},{8,7},{9,8},{10,9},{11,1... | collective-permute-start | bytes 6152 | tf_op jit(solution)/shard_map/ppermute | solution.py:17
  3.3 21.1 %collective-permute-start = (f32[2,256]{1,0:T(2,128)S(1)}, f32[2,256]{1,0:T(2,128)S(1)}, u32[]{:S(2)}, u32[]{:S(2)}) collective-permute-start(f32[2,256]{1,0:T(2,128)S(1)} %get-tuple-element.61), channel_id=1, source_target_pairs={{0,1},{1,2},{2,3},{3,4},{4,5},{5,6},{6,7},{7,8},{8,9},{9,10},{10,1... | collective-permute-start | bytes 6152 | tf_op jit(solution)/shard_map/ppermute | solution.py:14
  9.0 15.9 %collective-permute-start.3 = (f32[16,2,1,256]{3,2,1,0:T(1,128)S(1)}, f32[16,2,1,256]{3,2,1,0:T(1,128)S(1)}, u32[]{:S(2)}, u32[]{:S(2)}) collective-permute-start(f32[16,2,1,256]{3,2,1,0:T(1,128)S(1)} %get-tuple-element.45), channel_id=1, source_target_pairs={{1,0},{2,1},{3,2},{4,3},{5,4},{6,5},{7,6},{8,7},{9,8},{10,9},{11,1... | collective-permute-start | bytes 98312 | tf_op jit(solution)/shard_map/ppermute | solution.py:17
  10.9 14.0 %collective-permute-start.2 = (f32[16,2,1,256]{3,2,1,0:T(1,128)S(1)}, f32[16,2,1,256]{3,2,1,0:T(1,128)S(1)}, u32[]{:S(2)}, u32[]{:S(2)}) collective-permute-start(f32[16,2,1,256]{3,2,1,0:T(1,128)S(1)} %get-tuple-element.44), channel_id=1, source_target_pairs={{0,1},{1,2},{2,3},{3,4},{4,5},{5,6},{6,7},{7,8},{8,9},{9,10},{10,1... | collective-permute-start | bytes 98312 | tf_op jit(solution)/shard_map/ppermute | solution.py:14
  15.6 145.9 %collective-permute-start.9 = (f32[16,2,1,256]{3,2,1,0:T(1,128)S(1)}, f32[16,2,1,256]{3,2,1,0:T(1,128)S(1)}, u32[]{:S(2)}, u32[]{:S(2)}) collective-permute-start(f32[16,2,1,256]{3,2,1,0:T(1,128)S(1)} %get-tuple-element.35), channel_id=1, source_target_pairs={{1,0},{2,1},{3,2},{4,3},{5,4},{6,5},{7,6},{8,7},{9,8},{10,9},{11,1... | collective-permute-start | bytes 98312 | tf_op jit(solution)/shard_map/ppermute | solution.py:17
  17.6 0.7 copy-start.2
  17.6 1.0 copy-start.1
  18.7 0.7 copy-start.6
  19.4 0.7 copy-start.3
  20.0 0.7 copy-start.7
  20.8 140.8 %collective-permute-start.8 = (f32[16,2,1,256]{3,2,1,0:T(1,128)S(1)}, f32[16,2,1,256]{3,2,1,0:T(1,128)S(1)}, u32[]{:S(2)}, u32[]{:S(2)}) collective-permute-start(f32[16,2,1,256]{3,2,1,0:T(1,128)S(1)} %get-tuple-element.34), channel_id=1, source_target_pairs={{0,1},{1,2},{2,3},{3,4},{4,5},{5,6},{6,7},{7,8},{8,9},{9,10},{10,1... | collective-permute-start | bytes 98312 | tf_op jit(solution)/shard_map/ppermute | solution.py:14
  25.1 5.7 %collective-permute-start.5 = (f32[16,2,1,256]{3,2,1,0:T(1,128)S(1)}, f32[16,2,1,256]{3,2,1,0:T(1,128)S(1)}, u32[]{:S(2)}, u32[]{:S(2)}) collective-permute-start(f32[16,2,1,256]{3,2,1,0:T(1,128)S(1)} %get-tuple-element.41), channel_id=1, source_target_pairs={{1,0},{2,1},{3,2},{4,3},{5,4},{6,5},{7,6},{8,7},{9,8},{10,9},{11,1... | collective-permute-start | bytes 98312 | tf_op jit(solution)/shard_map/ppermute | solution.py:17
  27.1 4.7 %collective-permute-start.4 = (f32[16,2,1,256]{3,2,1,0:T(1,128)S(1)}, f32[16,2,1,256]{3,2,1,0:T(1,128)S(1)}, u32[]{:S(2)}, u32[]{:S(2)}) collective-permute-start(f32[16,2,1,256]{3,2,1,0:T(1,128)S(1)} %get-tuple-element.40), channel_id=1, source_target_pairs={{0,1},{1,2},{2,3},{3,4},{4,5},{5,6},{6,7},{7,8},{8,9},{9,10},{10,1... | collective-permute-start | bytes 98312 | tf_op jit(solution)/shard_map/ppermute | solution.py:14
  112.5 6.6 %collective-permute-start.7 = (f32[16,2,1,256]{3,2,1,0:T(1,128)S(1)}, f32[16,2,1,256]{3,2,1,0:T(1,128)S(1)}, u32[]{:S(2)}, u32[]{:S(2)}) collective-permute-start(f32[16,2,1,256]{3,2,1,0:T(1,128)S(1)} %get-tuple-element.37), channel_id=1, source_target_pairs={{1,0},{2,1},{3,2},{4,3},{5,4},{6,5},{7,6},{8,7},{9,8},{10,9},{11,1... | collective-permute-start | bytes 98312 | tf_op jit(solution)/shard_map/ppermute | solution.py:17
  117.0 3.1 %collective-permute-start.6 = (f32[16,2,1,256]{3,2,1,0:T(1,128)S(1)}, f32[16,2,1,256]{3,2,1,0:T(1,128)S(1)}, u32[]{:S(2)}, u32[]{:S(2)}) collective-permute-start(f32[16,2,1,256]{3,2,1,0:T(1,128)S(1)} %get-tuple-element.36), channel_id=1, source_target_pairs={{0,1},{1,2},{2,3},{3,4},{4,5},{5,6},{6,7},{7,8},{8,9},{9,10},{10,1... | collective-permute-start | bytes 98312 | tf_op jit(solution)/shard_map/ppermute | solution.py:14
  140.3 0.7 copy-start.4
  159.8 0.7 copy-start.5
  161.9 7.7 %collective-permute-start.11 = (f32[16,2,1,256]{3,2,1,0:T(1,128)S(1)}, f32[16,2,1,256]{3,2,1,0:T(1,128)S(1)}, u32[]{:S(2)}, u32[]{:S(2)}) collective-permute-start(f32[16,2,1,256]{3,2,1,0:T(1,128)S(1)} %get-tuple-element.29), channel_id=1, source_target_pairs={{1,0},{2,1},{3,2},{4,3},{5,4},{6,5},{7,6},{8,7},{9,8},{10,9},{11,1... | collective-permute-start | bytes 98312 | tf_op jit(solution)/shard_map/ppermute | solution.py:17
  164.0 5.6 %collective-permute-start.10 = (f32[16,2,1,256]{3,2,1,0:T(1,128)S(1)}, f32[16,2,1,256]{3,2,1,0:T(1,128)S(1)}, u32[]{:S(2)}, u32[]{:S(2)}) collective-permute-start(f32[16,2,1,256]{3,2,1,0:T(1,128)S(1)} %get-tuple-element.28), channel_id=1, source_target_pairs={{0,1},{1,2},{2,3},{3,4},{4,5},{5,6},{6,7},{7,8},{8,9},{9,10},{10,1... | collective-permute-start | bytes 98312 | tf_op jit(solution)/shard_map/ppermute | solution.py:14
  167.7 110.4 %collective-permute-start.15 = (f32[16,2,1,256]{3,2,1,0:T(1,128)S(1)}, f32[16,2,1,256]{3,2,1,0:T(1,128)S(1)}, u32[]{:S(2)}, u32[]{:S(2)}) collective-permute-start(f32[16,2,1,256]{3,2,1,0:T(1,128)S(1)} %slice.268), channel_id=1, source_target_pairs={{1,0},{2,1},{3,2},{4,3},{5,4},{6,5},{7,6},{8,7},{9,8},{10,9},{11,1... | collective-permute-start | bytes 98312 | tf_op jit(solution)/shard_map/ppermute | solution.py:25
  247.8 6.6 %collective-permute-start.13 = (f32[16,2,1,256]{3,2,1,0:T(1,128)S(1)}, f32[16,2,1,256]{3,2,1,0:T(1,128)S(1)}, u32[]{:S(2)}, u32[]{:S(2)}) collective-permute-start(f32[16,2,1,256]{3,2,1,0:T(1,128)S(1)} %get-tuple-element.25), channel_id=1, source_target_pairs={{1,0},{2,1},{3,2},{4,3},{5,4},{6,5},{7,6},{8,7},{9,8},{10,9},{11,1... | collective-permute-start | bytes 98312 | tf_op jit(solution)/shard_map/ppermute | solution.py:17
  252.4 3.1 %collective-permute-start.12 = (f32[16,2,1,256]{3,2,1,0:T(1,128)S(1)}, f32[16,2,1,256]{3,2,1,0:T(1,128)S(1)}, u32[]{:S(2)}, u32[]{:S(2)}) collective-permute-start(f32[16,2,1,256]{3,2,1,0:T(1,128)S(1)} %get-tuple-element.24), channel_id=1, source_target_pairs={{0,1},{1,2},{2,3},{3,4},{4,5},{5,6},{6,7},{7,8},{8,9},{9,10},{10,1... | collective-permute-start | bytes 98312 | tf_op jit(solution)/shard_map/ppermute | solution.py:14
  275.7 5.2 %collective-permute-start.14 = (f32[16,2,1,256]{3,2,1,0:T(1,128)S(1)}, f32[16,2,1,256]{3,2,1,0:T(1,128)S(1)}, u32[]{:S(2)}, u32[]{:S(2)}) collective-permute-start(f32[16,2,1,256]{3,2,1,0:T(1,128)S(1)} %slice.266), channel_id=1, source_target_pairs={{1,0},{2,1},{3,2},{4,3},{5,4},{6,5},{7,6},{8,7},{9,8},{10,9},{11,1... | collective-permute-start | bytes 98312 | tf_op jit(solution)/shard_map/ppermute | solution.py:25
